TPU v7x, 32 devices: a whole 2x2x4 slice. The times are simulated.
32 devices in a mesh: dp: 4 (over y, x), expert: 8 (over z, core).
Axes of the slice: x: 2, y: 2, z: 4, core: 2. Of those that a mesh axis runs over, the one named last changes fastest.
Arguments:
- hidden: bfloat16 [32, 2048], P(('dp', 'expert')), may hold values from -6 to 6
- attn_gain: float32 [2048], replicated, may hold values from 0.25 to 1.75
- query_weight: bfloat16 [3072, 2048], P('expert'), may hold values from -0.125 to 0.125
- latent_down: bfloat16 [2048, 576], replicated, may hold values from -0.125 to 0.125
- latent_up: bfloat16 [512, 4096], P(None, 'expert'), may hold values from -0.25 to 0.25
- out_weight: bfloat16 [2048, 2048], P('expert'), may hold values from -0.125 to 0.125
- latent_pool: bfloat16 [128, 32, 576], P('dp'), may hold values from -1000 to 1000
- page_table: int32 [32, 16], replicated, may hold values from -1 to 127, as said below
- page_counts: int32 [32], replicated, may hold values from 1 to 16, as said below
- ffn_gain: float32 [2048], replicated, may hold values from 0.25 to 1.75
- expert_ids: int32 [32, 6], replicated, may hold values from 0 to 23, all different within a row; in each aligned block of 32 rows (0 to 31, 32 to 63, ...) at most 16 rows name the same one
- expert_gates: float32 [32, 6], replicated, may hold values from 0.05 to 0.6
- old_place: int32 [8, 4], replicated, may hold values from 0 to 23, as said below
- new_place: int32 [8, 4], replicated, may hold values from 0 to 23, as said below
- expert_gate_up: bfloat16 [32, 2, 1408, 2048], P('expert', None, None, 'dp'), as said below
- expert_down: bfloat16 [32, 1408, 2048], P('expert', None, 'dp'), as said below
- shared_gate_up: bfloat16 [2, 2816, 2048], P(None, None, 'dp'), may hold values from -0.125 to 0.125
- shared_down: bfloat16 [2816, 2048], P(None, 'dp'), may hold values from -0.109375 to 0.109375
Outputs:
- layer_out: bfloat16 [32, 2048], P(('dp', 'expert'))
- moved_gate_up: bfloat16 [32, 2, 1408, 2048], P('expert', None, None, 'dp')
- moved_down: bfloat16 [32, 1408, 2048], P('expert', None, 'dp')
Inputs may be any that keep to these rules, and one draw needn't show every extreme that they name: `page_counts`: each request's count of cached pages; exactly one request has 16. `page_table`: row t names page_counts[t] pages of the pool, no page named twice in the table; its other entries are -1. Page p lies on dp index p // 32. `expert_ids`: no expert is named by more than 16 tokens in all; some expert by exactly 16. `old_place`: row i holds the experts of the slots on expert index i, slot s of row i being global slot i * 4 + s; every expert is held by one slot or more. `new_place`: equal to old_place except in exactly one slot of each row, which names another expert. `expert_gate_up`: slots that hold the same expert under old_place hold equal weights. `expert_down`: slots that hold the same expert under old_place hold equal weights.
All inputs are finite; a program needn't handle non-finite values.
Results may differ from a plain program's by a relative error of at most 0.02.
Values may be sent and summed in bfloat16 or wider, within the bound.
No kernel may reach another device: no remote copies, remote signals or barrier semaphores. Data moves between devices by JAX's collectives and lax.ppermute only.
A program may use at most 128 MiB of HBM per device.

v0:
```python
import math
import jax
import jax.numpy as jnp
from jax import lax
from jax.sharding import PartitionSpec as P

NOPE = 128
ROPE = 64
VHEAD = 128
LATENT = 512
EXP_DEV = 3
PAGE = 32
EPSILON = 1e-06
ROPE_BASE = 50000.0
MASKED_SCORE = -1e30
HIGHEST = lax.Precision.HIGHEST


def combined_all(part, axis, combine):
    gathered = jax.tree.map(lambda a: lax.all_gather(a, axis), part)

    def take(source):
        return jax.tree.map(lambda a: lax.dynamic_index_in_dim(a, source, 0, False), gathered)

    return lax.fori_loop(
        1, lax.axis_size(axis), lambda source, state: combine(state, take(source)), take(0)
    )


def rms_plain(values):
    mean_square = jnp.mean(values * values, axis=-1, keepdims=True)
    return values * lax.rsqrt(mean_square + EPSILON)


def rms_norm(values, norm_gain):
    return rms_plain(values) * norm_gain


def rotary(values, position):
    half_width = values.shape[-1] // 2
    exponent = jnp.arange(half_width).astype(jnp.float32) * (2.0 / values.shape[-1])
    frequency = jnp.exp(-exponent * math.log(ROPE_BASE))
    angles = position[..., None] * frequency
    cosine = jnp.cos(angles)
    sine_part = jnp.sin(angles)
    first_half = values[..., :half_width]
    second = values[..., half_width:]
    return jnp.concatenate(
        [first_half * cosine - second * sine_part, second * cosine + first_half * sine_part],
        axis=-1,
    )


def combine_parts(earlier, later):
    highest = jnp.maximum(earlier[0], later[0])
    weight_early = jnp.exp(earlier[0] - highest)
    weight_late = jnp.exp(later[0] - highest)
    return (
        highest,
        earlier[1] * weight_early + later[1] * weight_late,
        earlier[2] * weight_early[..., None] + later[2] * weight_late[..., None],
    )


def local(
    hidden,
    attn_gain,
    query_weight,
    latent_down,
    latent_up,
    out_weight,
    latent_pool,
    page_table,
    page_counts,
    ffn_gain,
    expert_ids,
    expert_gates,
    old_place,
    new_place,
    expert_gate_up,
    expert_down,
    shared_gate_up,
    shared_down,
):
    dp_count = lax.axis_size("dp")
    ex_count = lax.axis_size("expert")
    dp_index = lax.axis_index("dp")
    ex_index = lax.axis_index("expert")
    req_local = hidden.shape[0]
    group_rows = req_local * ex_count
    requests = page_counts.shape[0]
    head_local = query_weight.shape[0] // (NOPE + ROPE)
    score_scale = (NOPE + ROPE) ** (-0.5)
    group_start = dp_index * group_rows
    everyone = lax.all_gather(hidden, ("dp", "expert"), axis=0, tiled=True)
    normed = rms_norm(everyone.astype(jnp.float32), attn_gain).astype(jnp.bfloat16)
    queries = jnp.einsum(
        "td,qd->tq", normed, query_weight, preferred_element_type=jnp.float32
    ).reshape(requests, head_local, NOPE + ROPE)
    position = (page_counts * PAGE).astype(jnp.float32)
    query_rope = rotary(queries[..., NOPE:], position[:, None]).astype(jnp.bfloat16)
    up_table = latent_up.reshape(LATENT, head_local, NOPE + VHEAD)
    query_latent = jnp.einsum(
        "thn,lhn->thl",
        queries[..., :NOPE],
        up_table[..., :NOPE].astype(jnp.float32),
        precision=HIGHEST,
    ).astype(jnp.bfloat16)
    pages_local = latent_pool.shape[0]
    pool_total = pages_local * dp_count
    flat_pages = page_table.reshape(-1)
    flat_owner = jnp.repeat(jnp.arange(requests, dtype=jnp.int32), page_table.shape[1])
    target = jnp.where(flat_pages >= 0, flat_pages, pool_total)
    owner_all = jnp.full((pool_total,), -1, jnp.int32).at[target].set(flat_owner, mode="drop")
    page_owner = lax.dynamic_slice_in_dim(owner_all, dp_index * pages_local, pages_local)
    page_used = page_owner >= 0
    owner_safe = jnp.maximum(page_owner, 0)
    page_latent = latent_pool[..., :LATENT]
    page_rope = latent_pool[..., LATENT:]
    scores = jnp.einsum(
        "phl,pkl->phk", query_latent[owner_safe], page_latent, preferred_element_type=jnp.float32
    )
    scores = (
        scores
        + jnp.einsum(
            "phr,pkr->phk", query_rope[owner_safe], page_rope, preferred_element_type=jnp.float32
        )
    ) * score_scale
    raw_max = jnp.max(scores, axis=2)
    weights = jnp.exp(scores - raw_max[..., None])
    page_total = jnp.sum(weights, axis=2)
    page_mix = jnp.einsum(
        "phk,pkl->phl",
        weights.astype(jnp.bfloat16),
        page_latent,
        preferred_element_type=jnp.float32,
    )
    page_max = jnp.where(page_used[:, None], raw_max, MASKED_SCORE)
    member = page_owner[None, :] == jnp.arange(requests, dtype=jnp.int32)[:, None]
    req_max = jnp.max(jnp.where(member[:, :, None], page_max[None], MASKED_SCORE), axis=1)
    rescale = jnp.where(page_used[:, None], jnp.exp(page_max - req_max[owner_safe]), 0.0)
    member_float = member.astype(jnp.float32)
    req_total = jnp.dot(member_float, page_total * rescale, precision=HIGHEST)
    req_mix = jnp.einsum(
        "rp,phl->rhl", member_float, page_mix * rescale[..., None], precision=HIGHEST
    )
    merged = combined_all((req_max, req_total, req_mix), "dp", combine_parts)
    part_max = lax.dynamic_slice_in_dim(merged[0], group_start, group_rows, 0)
    part_total = lax.dynamic_slice_in_dim(merged[1], group_start, group_rows, 0)
    part_mix = lax.dynamic_slice_in_dim(merged[2], group_start, group_rows, 0)
    own_normed = lax.dynamic_slice_in_dim(normed, group_start, group_rows, 0)
    own_position = lax.dynamic_slice_in_dim(position, group_start, group_rows, 0)
    fresh_latent = jnp.dot(own_normed, latent_down, preferred_element_type=jnp.float32)
    new_latent = rms_plain(fresh_latent[:, :LATENT]).astype(jnp.bfloat16)
    new_rope = rotary(fresh_latent[:, LATENT:], own_position).astype(jnp.bfloat16)
    own_query = lax.dynamic_slice_in_dim(query_latent, group_start, group_rows, 0)
    own_rope_query = lax.dynamic_slice_in_dim(query_rope, group_start, group_rows, 0)
    own_score = jnp.einsum("thl,tl->th", own_query, new_latent, preferred_element_type=jnp.float32)
    own_score = (
        own_score
        + jnp.einsum("thr,tr->th", own_rope_query, new_rope, preferred_element_type=jnp.float32)
    ) * score_scale
    highest = jnp.maximum(part_max, own_score)
    kept_part = jnp.exp(part_max - highest)
    own_weight = jnp.exp(own_score - highest)
    denominator = part_total * kept_part + own_weight
    numerator = (
        part_mix * kept_part[..., None]
        + own_weight[..., None] * new_latent.astype(jnp.float32)[:, None, :]
    )
    attended = (numerator / denominator[..., None]).astype(jnp.bfloat16)
    heads_out = jnp.einsum(
        "thl,lhv->thv", attended, up_table[..., NOPE:], preferred_element_type=jnp.float32
    )
    heads_out = heads_out.astype(jnp.bfloat16).reshape(group_rows, head_local * VHEAD)
    partial_value = jnp.dot(heads_out, out_weight, preferred_element_type=jnp.float32)
    attn_out = lax.psum_scatter(partial_value, "expert", scatter_dimension=0, tiled=True)
    residual = hidden.astype(jnp.float32) + attn_out
    normed_ffn = rms_norm(residual, ffn_gain).astype(jnp.bfloat16)
    slots_local = expert_gate_up.shape[0]
    ff_width = expert_gate_up.shape[2]
    col_width = expert_gate_up.shape[3]
    every_row = lax.all_gather(normed_ffn, ("dp", "expert"), axis=0, tiled=True)
    my_columns = lax.dynamic_slice_in_dim(every_row, dp_index * col_width, col_width, 1)
    by_group = my_columns.reshape(dp_count, ex_count, req_local, col_width).transpose(1, 0, 2, 3)
    ffn_rows = by_group.reshape(requests, col_width)
    column_rows = lax.dynamic_index_in_dim(by_group, ex_index, 0, keepdims=False).reshape(
        dp_count * req_local, col_width
    )
    top_count = expert_ids.shape[1]
    experts_count = EXP_DEV * ex_count
    ids_order = (
        expert_ids.reshape(dp_count, ex_count, req_local, top_count)
        .transpose(1, 0, 2, 3)
        .reshape(requests, top_count)
    )
    gates_order = (
        expert_gates.reshape(dp_count, ex_count, req_local, top_count)
        .transpose(1, 0, 2, 3)
        .reshape(requests, top_count)
    )
    old_flat = old_place.reshape(-1)
    holds_map = old_flat[None, :] == jnp.arange(experts_count, dtype=jnp.int32)[:, None]
    holder = jnp.argmax(holds_map, axis=1)
    slot_of = holder[ids_order.reshape(-1)]
    capacity = 2 * requests * top_count // experts_count
    local_slot = slot_of - ex_index * slots_local
    slot_hot = local_slot[:, None] == jnp.arange(slots_local, dtype=jnp.int32)[None, :]
    slot_rank = jnp.cumsum(slot_hot.astype(jnp.int32), axis=0) - 1
    position_in = jnp.where(slot_hot, slot_rank, capacity)
    route_hot = (
        position_in[:, :, None] == jnp.arange(capacity, dtype=jnp.int32)[None, None, :]
    ).astype(jnp.float32)
    route_hot = route_hot.reshape(requests, top_count, slots_local, capacity)
    dispatch = jnp.sum(route_hot, axis=1).astype(jnp.bfloat16)
    combine = jnp.sum(route_hot * gates_order[:, :, None, None], axis=1)
    slot_inputs = jnp.einsum(
        "tsc,td->scd", dispatch, ffn_rows, preferred_element_type=jnp.float32
    ).astype(jnp.bfloat16)
    routed_part = jnp.einsum(
        "scd,sgfd->sgcf", slot_inputs, expert_gate_up, preferred_element_type=jnp.float32
    )
    shared_part = jnp.einsum(
        "td,gfd->gtf", column_rows, shared_gate_up, preferred_element_type=jnp.float32
    )
    routed_sum, shared_sum = lax.psum((routed_part, shared_part), "dp")
    activated = (jax.nn.silu(routed_sum[:, 0]) * routed_sum[:, 1]).astype(jnp.bfloat16)
    slot_out = jnp.einsum(
        "scf,sfd->scd", activated, expert_down, preferred_element_type=jnp.float32
    )
    routed = jnp.einsum("tsc,scd->td", combine, slot_out, precision=HIGHEST)
    shared_act = (jax.nn.silu(shared_sum[0]) * shared_sum[1]).astype(jnp.bfloat16)
    shared_term = jnp.dot(shared_act, shared_down, preferred_element_type=jnp.float32)
    moe_rows = lax.psum_scatter(routed, "expert", scatter_dimension=0, tiled=True)
    moe_part = lax.all_to_all(moe_rows + shared_term, "dp", split_axis=0, concat_axis=1, tiled=True)
    layer_out = (residual + moe_part).astype(jnp.bfloat16)
    changed = old_place != new_place
    moved_slot = jnp.argmax(changed, axis=1)
    wanted_expert = jnp.take_along_axis(new_place, moved_slot[:, None], axis=1)[:, 0]
    source = holder[wanted_expert]
    stacked_gate_up = expert_gate_up.reshape(slots_local, 2 * ff_width, col_width)
    spread = (
        lax.all_to_all(stacked_gate_up, "expert", split_axis=1, concat_axis=0, tiled=True),
        lax.all_to_all(expert_down, "expert", split_axis=1, concat_axis=0, tiled=True),
    )
    outgoing = (spread[0][source], spread[1][source])
    arrived = (
        lax.all_to_all(outgoing[0], "expert", split_axis=0, concat_axis=1, tiled=True),
        lax.all_to_all(outgoing[1], "expert", split_axis=0, concat_axis=1, tiled=True),
    )
    arrived_gate_up = arrived[0].reshape(1, 2, ff_width, col_width)
    my_slot = moved_slot[ex_index]
    is_moved = jnp.arange(slots_local, dtype=jnp.int32) == my_slot
    moved_gate_up = jnp.where(is_moved[:, None, None, None], arrived_gate_up, expert_gate_up)
    moved_down = jnp.where(is_moved[:, None, None], arrived[1], expert_down)
    return (layer_out, moved_gate_up, moved_down)


def solution(mesh):
    in_specs = (
        P(("dp", "expert"), None),
        P(),
        P("expert", None),
        P(),
        P(None, "expert"),
        P("expert", None),
        P("dp", None, None),
        P(),
        P(),
        P(),
        P(),
        P(),
        P(),
        P(),
        P("expert", None, None, "dp"),
        P("expert", None, "dp"),
        P(None, None, "dp"),
        P(None, "dp"),
    )
    out_specs = (P(("dp", "expert"), None), P("expert", None, None, "dp"), P("expert", None, "dp"))
    return jax.shard_map(local, mesh=mesh, in_specs=in_specs, out_specs=out_specs, check_vma=False)
```

profile of v0, /device:TPU:0, one launch (start us, length us, event | category | flops | bytes accessed | tf_op | source)
XLA Modules:
  0.0 888.6 jit_solution(454954826351109402)
XLA Ops:
  12.6 44.5 %all-gather.3 = bf16[32,1,2048]{2,1,0:T(2,128)(2,1)S(1)} all-gather(bf16[1,1,2048]{2,1,0:T(2,128)(2,1)} %bitcast.231), channel_id=1, replica_groups=mesh['dp'=4,'expert'=8] {'dp','expert'}, dimensions={0}, use_global_device_ids=true | all-gather | bytes 135168 | tf_op jit(solution)/shard_map/all_gather | solution.py:95
  76.5 9.4 %all-gather.2 = f32[128,2,512]{2,0,1:T(8,128)S(1)} all-gather(f32[32,2,512]{2,0,1:T(8,128)S(1)} %fusion.24), channel_id=4, replica_groups=mesh['dp'=4,'expert'=8] {'dp'}, dimensions={0}, use_global_device_ids=true | all-gather | bytes 655360 | tf_op jit(solution)/shard_map/all_gather | solution.py:20
  86.2 8.6 all-gather.5
  96.0 7.6 all-gather.4
  104.8 13.2 %while.19 = (s32[]{:T(128)}, f32[32,2]{0,1:T(2,128)}, f32[32,2]{0,1:T(2,128)}, f32[32,2,512]{2,1,0:T(2,128)S(1)}, f32[4,32,2]{1,2,0:T(2,128)}, /*index=5*/f32[4,...) while((s32[]{:T(128)}, f32[32,2]{0,1:T(2,128)}, f32[32,2]{0,1:T(2,128)}, ...), condition=%wide.region_6.7_spmd, body=%wide.region_5.6_spmd.sunk | while | flops 98693 | bytes 659095 | solution.py:25
  136.4 4.4 compare_select_fusion.3
  140.9 10.5 %select_subtract_fusion = s32[192]{0:T(256)S(1)} fusion(pred[192]{0:T(512)(128)(4,1)S(1)} %get-tuple-element.241, pred[192]{0:T(512)(128)(4,1)S(1)} %get-tuple-element.240, pred[192]{0:T(512)(128)(4,1)S(1)} %get-tuple-element.239, pred[192]{0:T(512)(128)(4,1)S(1)} %get-tuple-element.238, pred[192]{0:T(512)(128)(4,1)S(1)} %get-tuple-element.237, ...), kind=kLoop, calls=%fused_computation.178 | loop fusion | flops 3456 | bytes 4872 | tf_op jit(solution)/shard_map/sub | solution.py:207
  155.6 28.0 %all-reduce.8.cloned.1.call-done = f32[8,2048]{1,0:T(8,128)} async-done(((f32[8,2048]{1,0:T(8,128)}), f32[8,2048]{1,0:T(8,128)}) %all-reduce.8.cloned.1.call-update) | async-done | bytes 65552
  187.1 40.5 %all-gather.6 = bf16[32,1,2048]{2,1,0:T(2,128)(2,1)S(1)} all-gather(bf16[1,1,2048]{2,1,0:T(2,128)(2,1)S(1)} %convert_bitcast_fusion), channel_id=1, replica_groups=mesh['dp'=4,'expert'=8] {'dp','expert'}, dimensions={0}, use_global_device_ids=true | all-gather | bytes 135168 | tf_op jit(solution)/shard_map/all_gather | solution.py:183
  227.8 4.9 convolution_bitcast_fusion
  232.7 6.9 convolution_bitcast_fusion.1
  239.6 45.8 %all-reduce.12.cloned.1.call-done = (f32[2,4,2816]{2,1,0:T(4,128)}, f32[4,2,16,1408]{3,2,1,0:T(8,128)}) async-done(((f32[2,4,2816]{2,1,0:T(4,128)}, f32[4,2,16,1408]{3,2,1,0:T(8,128)}), (f32[2,4,2816]{2,1,0:T(4,128)}, f32[4,2,16,1408]{3,2,1,0:T(8,128)})) %all-reduce.12.cloned.1.call-update) | async-done | bytes 811024 | tf_op jit(solution)/shard_map/psum | solution.py:226
  285.4 3.8 fusion.21
  290.8 53.2 %all-reduce.10.cloned.1.call-done = f32[32,512]{1,0:T(8,128)} async-done(((f32[32,512]{1,0:T(8,128)}), f32[32,512]{1,0:T(8,128)}) %all-reduce.10.cloned.1.call-update) | async-done | bytes 65552
  345.8 3.6 all-to-all-start
  349.4 23.9 %copy.152 = bf16[4,1408,512]{2,0,1:T(4,128)(2,1)} copy(bf16[4,1408,512]{2,1,0:T(8,128)(2,1)} %param.35) | data formatting | bytes 11534336 | tf_op args[15]
  373.3 4.7 all-to-all-start.3
  378.0 14.4 %copy.149 = bf16[4,2,1408,512]{3,0,2,1:T(4,128)(2,1)} copy(bf16[4,2,1408,512]{3,2,1,0:T(8,128)(2,1)} %param.34) | data formatting | bytes 23068672 | tf_op args[14]
  392.4 113.3 %all-to-all-done.3 = bf16[4,1408,512]{2,0,1:T(4,128)(2,1)} async-done(((bf16[4,1408,512]{2,0,1:T(4,128)(2,1)}), bf16[4,1408,512]{2,0,1:T(4,128)(2,1)}, u32[]{:S(2)}, u32[]{:S(2)}) %all-to-all-start.3) | async-done | bytes 5767200 | tf_op jit(solution)/shard_map/all_to_all | solution.py:244
  505.7 5.4 all-to-all-start.1
  513.0 3.8 copy.153
  519.7 4.4 gather_fusion.5
  524.1 238.3 %all-to-all-done.1 = bf16[4,2816,512]{2,0,1:T(4,128)(2,1)} async-done(((bf16[4,2816,512]{2,0,1:T(4,128)(2,1)}), bf16[4,2816,512]{2,0,1:T(4,128)(2,1)}, u32[]{:S(2)}, u32[]{:S(2)}) %all-to-all-start.1) | async-done | bytes 11534368 | tf_op jit(solution)/shard_map/all_to_all | solution.py:243
  762.4 3.6 all-to-all-start.4
  766.0 7.9 copy.150
  773.9 5.1 copy.151
  779.0 6.6 gather_fusion.4
  785.5 15.4 %all-to-all-done.4 = bf16[8,176,512]{2,1,0:T(8,128)(2,1)S(1)} async-done(((bf16[8,176,512]{2,1,0:T(8,128)(2,1)}), bf16[8,176,512]{2,1,0:T(8,128)(2,1)S(1)}, u32[]{:S(2)}, u32[]{:S(2)}) %all-to-all-start.4) | async-done | bytes 1441824 | tf_op jit(solution)/shard_map/all_to_all | solution.py:249
  800.9 4.4 all-to-all-start.2
  807.2 5.8 broadcast_select_fusion.1
  813.0 58.2 %all-to-all-done.2 = bf16[8,352,512]{2,1,0:T(8,128)(2,1)} async-done(((bf16[8,352,512]{2,1,0:T(8,128)(2,1)}), bf16[8,352,512]{2,1,0:T(8,128)(2,1)}, u32[]{:S(2)}, u32[]{:S(2)}) %all-to-all-start.2) | async-done | bytes 2883616 | tf_op jit(solution)/shard_map/all_to_all | solution.py:248
  871.3 10.8 %broadcast_select_fusion = bf16[4,2,1408,512]{3,2,1,0:T(8,128)(2,1)} fusion(bf16[4,2,1408,512]{3,2,1,0:T(8,128)(2,1)} %param.34, pred[4]{0:T(512)(128)(4,1)S(1)} %iota_compare_fusion.7, bf16[2,1408,512]{2,1,0:T(8,128)(2,1)} %bitcast.74), kind=kLoop, calls=%fused_computation.19 | loop fusion | flops 5767168 | bytes 25952260 | tf_op jit(solution)/shard_map/jit(_where)/select_n | solution.py:254
  (168 shorter events, 75.4 us)
Async XLA Ops:
  7.2 336.8 %copy-start = (bf16[2816,512]{1,0:T(8,128)(2,1)S(1)}, bf16[2816,512]{1,0:T(8,128)(2,1)}, u32[]{:S(2)}) copy-start(bf16[2816,512]{1,0:T(8,128)(2,1)} %param.37) | copy-start | bytes 8650756
  7.2 53.9 %copy-start.15 = (s32[32]{0:T(128)S(1)}, s32[32]{0:T(128)}, u32[]{:S(2)}) copy-start(s32[32]{0:T(128)} %param.28) | copy-start | bytes 388
  7.2 176.4 %all-reduce.8.cloned.1.call-start = ((), (), s32[]{:S(2)}) async-start(), calls=%async_computation.5 | async-start | bytes 131072
  7.3 58.0 %copy-start.14 = (f32[32]{0:T(128)}, f32[32]{0:T(128)S(1)}, u32[]{:S(2)}) copy-start(f32[32]{0:T(128)S(1)} %multiply_exponential_fusion) | copy-start | bytes 388
  11.5 0.5 copy-start.10
  58.4 0.7 copy-start.5
  63.0 13.2 %copy-start.3 = (bf16[512,512]{0,1:T(8,128)(2,1)}, bf16[512,512]{0,1:T(8,128)(2,1)S(1)}, u32[]{:S(2)}) copy-start(bf16[512,512]{0,1:T(8,128)(2,1)S(1)} %copy.126) | copy-start | bytes 1572868
  66.2 0.6 copy-start.7
  66.2 0.6 copy-start.8
  68.4 7.8 copy-start.11
  71.3 14.6 %copy-start.12 = (s32[32]{0:T(128)S(1)}, s32[32]{0:T(128)}, u32[]{:S(2)}) copy-start(s32[32]{0:T(128)} %copy-done.10) | copy-start | bytes 388
  118.1 12.1 %copy-start.4 = (bf16[512,512]{0,1:T(8,128)(2,1)S(1)}, bf16[512,512]{0,1:T(8,128)(2,1)}, u32[]{:S(2)}) copy-start(bf16[512,512]{0,1:T(8,128)(2,1)} %copy-done.3) | copy-start | bytes 1572868
  120.5 0.6 copy-start.6
  132.5 153.0 %all-reduce.12.cloned.1.call-start = ((), (), s32[]{:S(2)}) async-start(), calls=%async_computation.7 | async-start | bytes 1622016 | tf_op jit(solution)/shard_map/psum | solution.py:226
  239.6 104.4 %all-reduce.10.cloned.1.call-start = ((), (), s32[]{:S(2)}) async-start(), calls=%async_computation.6 | async-start | bytes 131072
  285.4 58.5 %copy-start.9 = (f32[2,4,2816]{2,1,0:T(4,128)S(1)}, f32[2,4,2816]{2,1,0:T(4,128)}, u32[]{:S(2)}) copy-start(f32[2,4,2816]{2,1,0:T(4,128)} %get-tuple-element.256) | copy-start | bytes 270340
  345.8 27.5 %all-to-all-start = ((f32[4,1,512]{2,1,0:T(1,128)}), f32[4,1,512]{2,1,0:T(1,128)S(1)}, u32[]{:S(2)}, u32[]{:S(2)}) async-start(f32[4,1,512]{2,1,0:T(1,128)} %copy.148), calls=%async_computation | async-start | bytes 16384 | tf_op jit(solution)/shard_map/all_to_all | solution.py:235
  373.3 132.4 %all-to-all-start.3 = ((bf16[4,1408,512]{2,0,1:T(4,128)(2,1)}), bf16[4,1408,512]{2,0,1:T(4,128)(2,1)}, u32[]{:S(2)}, u32[]{:S(2)}) async-start(bf16[4,1408,512]{2,0,1:T(4,128)(2,1)} %copy.152), calls=%async_computation.3 | async-start | bytes 11534336 | tf_op jit(solution)/shard_map/all_to_all | solution.py:244
  505.7 5.4 copy-start.2
  505.7 5.4 copy-start.13
  505.7 256.7 %all-to-all-start.1 = ((bf16[4,2816,512]{2,0,1:T(4,128)(2,1)}), bf16[4,2816,512]{2,0,1:T(4,128)(2,1)}, u32[]{:S(2)}, u32[]{:S(2)}) async-start(bf16[4,2816,512]{2,0,1:T(4,128)(2,1)} %bitcast.217), calls=%async_computation.1 | async-start | bytes 23068672 | tf_op jit(solution)/shard_map/all_to_all | solution.py:243
  762.4 38.5 %all-to-all-start.4 = ((bf16[8,176,512]{2,1,0:T(8,128)(2,1)}), bf16[8,176,512]{2,1,0:T(8,128)(2,1)S(1)}, u32[]{:S(2)}, u32[]{:S(2)}) async-start(bf16[8,176,512]{2,1,0:T(8,128)(2,1)} %gather_fusion.5), calls=%async_computation.4 | async-start | bytes 2883584 | tf_op jit(solution)/shard_map/all_to_all | solution.py:249
  800.9 70.4 %all-to-all-start.2 = ((bf16[8,352,512]{2,1,0:T(8,128)(2,1)}), bf16[8,352,512]{2,1,0:T(8,128)(2,1)}, u32[]{:S(2)}, u32[]{:S(2)}) async-start(bf16[8,352,512]{2,1,0:T(8,128)(2,1)} %gather_fusion.4), calls=%async_computation.2 | async-start | bytes 5767168 | tf_op jit(solution)/shard_map/all_to_all | solution.py:248
  871.3 10.8 %copy-start.1 = (bf16[2816,512]{1,0:T(8,128)(2,1)S(1)}, bf16[2816,512]{1,0:T(8,128)(2,1)}, u32[]{:S(2)}) copy-start(bf16[2816,512]{1,0:T(8,128)(2,1)} %param.37) | copy-start | bytes 8650756
Sparse Core Ops, SparseCore 0:
  132.6 50.9 all-reduce.7
  239.7 45.6 all-reduce.11
  290.2 53.6 all-reduce.9
where the time goes:
time: 891 us; the launch traced here: 889 us
  waiting for transfers between devices  552 us (62%)
  blocking collectives  111 us (12%)
  local copies, waits for them, and re-layouts  100 us (11%)
  other arithmetic  57 us (6%)
  matrix products  31 us (3%)
  starting transfers between devices  21.9 us (2%)
  between operations  15.5 us (2%)
    all_to_all x1, waiting for transfers between devices, local(): lax.all_to_all(stacked_gate_up, 'expert', split_axis=1, concat_axis=0, ti...  238 us
    all_to_all x1, waiting for transfers between devices, local(): lax.all_to_all(expert_down, 'expert', split_axis=1, concat_axis=0, tiled=...  113 us
    unnamed x5, waiting for transfers between devices  81.2 us
    all_to_all x1, waiting for transfers between devices, local(): lax.all_to_all(outgoing[0], 'expert', split_axis=0, concat_axis=1, tiled=...  58.2 us
    psum x1, waiting for transfers between devices, local(): routed_sum, shared_sum = lax.psum((routed_part, shared_part), 'dp')  45.8 us
    unnamed x41, local copies, waits for them, and re-layouts  44.8 us
    all_gather x1, blocking collectives, local(): everyone = lax.all_gather(hidden, ('dp', 'expert'), axis=0, tiled=True)  44.5 us
    all_gather x1, blocking collectives, local(): every_row = lax.all_gather(normed_ffn, ('dp', 'expert'), axis=0, tiled=True)  40.5 us
  transfers between devices with their start and end apart: 8, of which 7 were waited for; matrix products, arithmetic and copies ran while one was open for 11% of the time, Pallas kernels for 0%

commit v1 on v0

--- a/solution.py
+++ b/solution.py
@@ -82,6 +82,27 @@
     shared_gate_up,
     shared_down,
 ):
+
+    def try_all_the_strings(t0, dim_i, at_axis=0):
+        ready = jax.lax.axis_size("expert")
+        base_arr, wide_out = (ready, jax.lax.axis_index("expert"))
+        v1 = t0.shape[dim_i] // base_arr
+        h_now = list(t0.shape)
+        h_now[dim_i] = v1
+        carry_in = h_now[at_axis]
+        h_now[at_axis] = carry_in * base_arr
+        newest = jnp.zeros(h_now, t0.dtype)
+        for no in range(base_arr):
+            near = lax.dynamic_slice_in_dim(t0, (wide_out ^ no) * v1, v1, axis=dim_i)
+            if no:
+                now = map(lambda k: (k, k ^ no), range(base_arr))
+                fresh = list(now)
+                near = jax.lax.ppermute(near, axis_name="expert", perm=fresh)
+            newest = lax.dynamic_update_slice_in_dim(
+                newest, near, (wide_out ^ no) * carry_in, axis=at_axis
+            )
+        return newest
+
     dp_count = lax.axis_size("dp")
     ex_count = lax.axis_size("expert")
     dp_index = lax.axis_index("dp")
@@ -241,7 +262,7 @@
     stacked_gate_up = expert_gate_up.reshape(slots_local, 2 * ff_width, col_width)
     spread = (
         lax.all_to_all(stacked_gate_up, "expert", split_axis=1, concat_axis=0, tiled=True),
-        lax.all_to_all(expert_down, "expert", split_axis=1, concat_axis=0, tiled=True),
+        try_all_the_strings(expert_down, 1),
     )
     outgoing = (spread[0][source], spread[1][source])
     arrived = (

time: 891 us -> 857 us (0.962)
  starting transfers between devices: 21.9 us -> 55.6 us
  waiting for transfers between devices: 552 us -> 519 us
  local copies, waits for them, and re-layouts: 100 us -> 78.9 us
  other arithmetic: 57 us -> 47.3 us
    ppermute x0 -> x7, waiting for transfers between devices: none -> 316 us  [try_all_the_strings(): near = jax.lax.ppermute(near, axis_name='expert', perm=fresh)]
    all_to_all x1, waiting for transfers between devices: 238 us -> 0.01 us  [local(): lax.all_to_all(stacked_gate_up, 'expert', split_axis=1, concat_axis=0, ti...]
    all_to_all x1 -> x0, waiting for transfers between devices: 113 us -> none  [local(): lax.all_to_all(expert_down, 'expert', split_axis=1, concat_axis=0, tiled=...]
    all_to_all x1, starting transfers between devices: 3.58 us -> 31.1 us  [local(): lax.all_to_all(outgoing[1], 'expert', split_axis=0, concat_axis=1, tiled=...]
    unnamed x41 -> x46, local copies, waits for them, and re-layouts: 44.8 us -> 20 us
    ppermute x0 -> x7, starting transfers between devices: none -> 10.8 us  [try_all_the_strings(): near = jax.lax.ppermute(near, axis_name='expert', perm=fresh)]
  transfers between devices with their start and end apart: 8 -> 14, of which waited for: 7 -> 9; matrix products, arithmetic and copies ran while one was open for 11% -> 10% of each run, Pallas kernels for 0% -> 0%
where the time goes in v1:
time: 857 us; the launch traced here: 855 us
  waiting for transfers between devices  519 us (61%)
  blocking collectives  109 us (13%)
  local copies, waits for them, and re-layouts  78.9 us (9%)
  starting transfers between devices  55.6 us (6%)
  other arithmetic  47.3 us (6%)
  matrix products  29.7 us (3%)
  between operations  15.6 us (2%)
    ppermute x7, waiting for transfers between devices, try_all_the_strings(): near = jax.lax.ppermute(near, axis_name='expert', perm=fresh)  316 us
    unnamed x5, waiting for transfers between devices  82.6 us
    all_to_all x1, waiting for transfers between devices, local(): lax.all_to_all(outgoing[0], 'expert', split_axis=0, concat_axis=1, tiled=...  58.3 us
    psum x1, waiting for transfers between devices, local(): routed_sum, shared_sum = lax.psum((routed_part, shared_part), 'dp')  45.8 us
    all_gather x1, blocking collectives, local(): everyone = lax.all_gather(hidden, ('dp', 'expert'), axis=0, tiled=True)  44.5 us
    all_gather x1, blocking collectives, local(): every_row = lax.all_gather(normed_ffn, ('dp', 'expert'), axis=0, tiled=True)  40.5 us
    all_to_all x1, starting transfers between devices, local(): lax.all_to_all(outgoing[1], 'expert', split_axis=0, concat_axis=1, tiled=...  31.1 us
    all_gather x3, blocking collectives, combined_all(): gathered = jax.tree.map(lambda a: lax.all_gather(a, axis), part)  24.2 us
  transfers between devices with their start and end apart: 14, of which 9 were waited for; matrix products, arithmetic and copies ran while one was open for 10% of the time, Pallas kernels for 0%

profile of v1, /device:TPU:0, one launch (start us, length us, event | category | flops | bytes accessed | tf_op | source)
XLA Modules:
  0.0 855.0 jit_solution(16270287530988068560)
XLA Ops:
  13.3 44.5 %all-gather.3 = bf16[32,1,2048]{2,1,0:T(2,128)(2,1)S(1)} all-gather(bf16[1,1,2048]{2,1,0:T(2,128)(2,1)} %bitcast.225), channel_id=1, replica_groups=mesh['dp'=4,'expert'=8] {'dp','expert'}, dimensions={0}, use_global_device_ids=true | all-gather | bytes 135168 | tf_op jit(solution)/shard_map/all_gather | solution.py:116
  74.9 7.1 all-gather.4
  85.3 8.1 all-gather.5
  93.6 9.0 %all-gather.2 = f32[128,2,512]{2,0,1:T(8,128)S(1)} all-gather(f32[32,2,512]{2,0,1:T(8,128)S(1)} %fusion.24), channel_id=4, replica_groups=mesh['dp'=4,'expert'=8] {'dp'}, dimensions={0}, use_global_device_ids=true | all-gather | bytes 655360 | tf_op jit(solution)/shard_map/all_gather | solution.py:20
  103.4 4.2 while.19
  118.3 4.4 compare_select_fusion.3
  122.9 10.5 %select_subtract_fusion = s32[192]{0:T(256)S(1)} fusion(pred[192]{0:T(512)(128)(4,1)S(1)} %get-tuple-element.241, pred[192]{0:T(512)(128)(4,1)S(1)} %get-tuple-element.240, pred[192]{0:T(512)(128)(4,1)S(1)} %get-tuple-element.239, pred[192]{0:T(512)(128)(4,1)S(1)} %get-tuple-element.238, pred[192]{0:T(512)(128)(4,1)S(1)} %get-tuple-element.237, ...), kind=kLoop, calls=%fused_computation.192 | loop fusion | flops 3456 | bytes 4872 | tf_op jit(solution)/shard_map/sub | solution.py:228
  136.2 29.4 %all-reduce.8.cloned.1.call-done = f32[8,2048]{1,0:T(8,128)} async-done(((f32[8,2048]{1,0:T(8,128)}), f32[8,2048]{1,0:T(8,128)}) %all-reduce.8.cloned.1.call-update) | async-done | bytes 65552
  168.4 40.5 %all-gather.6 = bf16[32,1,2048]{2,1,0:T(2,128)(2,1)S(1)} all-gather(bf16[1,1,2048]{2,1,0:T(2,128)(2,1)S(1)} %convert_bitcast_fusion), channel_id=1, replica_groups=mesh['dp'=4,'expert'=8] {'dp','expert'}, dimensions={0}, use_global_device_ids=true | all-gather | bytes 135168 | tf_op jit(solution)/shard_map/all_gather | solution.py:204
  209.2 4.9 convolution_bitcast_fusion
  214.0 6.9 convolution_bitcast_fusion.1
  221.0 45.8 %all-reduce.12.cloned.1.call-done = (f32[2,4,2816]{2,1,0:T(4,128)}, f32[4,2,16,1408]{3,2,1,0:T(8,128)}) async-done(((f32[2,4,2816]{2,1,0:T(4,128)}, f32[4,2,16,1408]{3,2,1,0:T(8,128)}), (f32[2,4,2816]{2,1,0:T(4,128)}, f32[4,2,16,1408]{3,2,1,0:T(8,128)})) %all-reduce.12.cloned.1.call-update) | async-done | bytes 811024 | tf_op jit(solution)/shard_map/psum | solution.py:247
  266.8 3.8 fusion.21
  272.1 53.2 %all-reduce.10.cloned.1.call-done = f32[32,512]{1,0:T(8,128)} async-done(((f32[32,512]{1,0:T(8,128)}), f32[32,512]{1,0:T(8,128)}) %all-reduce.10.cloned.1.call-update) | async-done | bytes 65552
  327.1 3.6 all-to-all-start
  330.7 14.4 %copy.145 = bf16[4,2,1408,512]{3,0,2,1:T(4,128)(2,1)} copy(bf16[4,2,1408,512]{3,2,1,0:T(8,128)(2,1)} %param.34) | data formatting | bytes 23068672 | tf_op args[14]
  345.2 5.4 all-to-all-start.1
  353.8 5.2 constant_dynamic-slice_fusion.2
  369.3 183.5 %collective-permute-done.1 = bf16[4,176,512]{2,1,0:T(8,128)(2,1)} collective-permute-done((bf16[4,176,512]{2,1,0:T(8,128)(2,1)}, bf16[4,176,512]{2,1,0:T(8,128)(2,1)}, u32[]{:S(2)}, u32[]{:S(2)}) %collective-permute-start.1) | collective-permute-done | bytes 720928 | tf_op jit(solution)/shard_map/ppermute | solution.py:100
  559.4 8.9 %collective-permute-done.2 = bf16[4,176,512]{2,1,0:T(8,128)(2,1)S(1)} collective-permute-done((bf16[4,176,512]{2,1,0:T(8,128)(2,1)}, bf16[4,176,512]{2,1,0:T(8,128)(2,1)S(1)}, u32[]{:S(2)}, u32[]{:S(2)}) %collective-permute-start.2) | collective-permute-done | bytes 720928 | tf_op jit(solution)/shard_map/ppermute | solution.py:100
  569.2 110.3 %collective-permute-done.3 = bf16[4,176,512]{2,1,0:T(8,128)(2,1)S(1)} collective-permute-done((bf16[4,176,512]{2,1,0:T(8,128)(2,1)}, bf16[4,176,512]{2,1,0:T(8,128)(2,1)S(1)}, u32[]{:S(2)}, u32[]{:S(2)}) %collective-permute-start.3) | collective-permute-done | bytes 720928 | tf_op jit(solution)/shard_map/ppermute | solution.py:100
  680.4 13.6 %collective-permute-done.4 = bf16[4,176,512]{2,1,0:T(8,128)(2,1)S(1)} collective-permute-done((bf16[4,176,512]{2,1,0:T(8,128)(2,1)}, bf16[4,176,512]{2,1,0:T(8,128)(2,1)S(1)}, u32[]{:S(2)}, u32[]{:S(2)}) %collective-permute-start.4) | collective-permute-done | bytes 720928 | tf_op jit(solution)/shard_map/ppermute | solution.py:100
  696.7 4.4 gather_fusion.5
  701.1 31.1 %all-to-all-start.3 = ((bf16[8,176,512]{2,1,0:T(8,128)(2,1)}), bf16[8,176,512]{2,1,0:T(8,128)(2,1)S(1)}, u32[]{:S(2)}, u32[]{:S(2)}) async-start(bf16[8,176,512]{2,1,0:T(8,128)(2,1)} %gather_fusion.5), calls=%async_computation.3 | async-start | bytes 2883584 | tf_op jit(solution)/shard_map/all_to_all | solution.py:270
  732.3 7.9 copy.146
  740.2 5.1 copy.147
  745.3 6.6 gather_fusion.4
  751.9 15.4 %all-to-all-done.3 = bf16[8,176,512]{2,1,0:T(8,128)(2,1)S(1)} async-done(((bf16[8,176,512]{2,1,0:T(8,128)(2,1)}), bf16[8,176,512]{2,1,0:T(8,128)(2,1)S(1)}, u32[]{:S(2)}, u32[]{:S(2)}) %all-to-all-start.3) | async-done | bytes 1441824 | tf_op jit(solution)/shard_map/all_to_all | solution.py:270
  767.3 4.4 all-to-all-start.2
  773.6 5.8 broadcast_select_fusion.1
  779.4 58.3 %all-to-all-done.2 = bf16[8,352,512]{2,1,0:T(8,128)(2,1)} async-done(((bf16[8,352,512]{2,1,0:T(8,128)(2,1)}), bf16[8,352,512]{2,1,0:T(8,128)(2,1)}, u32[]{:S(2)}, u32[]{:S(2)}) %all-to-all-start.2) | async-done | bytes 2883616 | tf_op jit(solution)/shard_map/all_to_all | solution.py:269
  837.7 10.8 %broadcast_select_fusion = bf16[4,2,1408,512]{3,2,1,0:T(8,128)(2,1)} fusion(bf16[4,2,1408,512]{3,2,1,0:T(8,128)(2,1)} %param.34, pred[4]{0:T(512)(128)(4,1)S(1)} %iota_compare_fusion.7, bf16[2,1408,512]{2,1,0:T(8,128)(2,1)} %bitcast.74), kind=kLoop, calls=%fused_computation.19 | loop fusion | flops 5767168 | bytes 25952260 | tf_op jit(solution)/shard_map/jit(_where)/select_n | solution.py:275
  (192 shorter events, 76.3 us)
Async XLA Ops:
  7.2 318.1 %copy-start = (bf16[2816,512]{1,0:T(8,128)(2,1)S(1)}, bf16[2816,512]{1,0:T(8,128)(2,1)}, u32[]{:S(2)}) copy-start(bf16[2816,512]{1,0:T(8,128)(2,1)} %param.37) | copy-start | bytes 8650756
  7.2 158.4 %all-reduce.8.cloned.1.call-start = ((), (), s32[]{:S(2)}) async-start(), calls=%async_computation.4 | async-start | bytes 131072
  11.5 63.3 %copy-start.16 = (pred[32]{0:T(512)(128)(4,1)}, pred[32]{0:T(512)(128)(4,1)S(1)}, u32[]{:S(2)}) copy-start(pred[32]{0:T(512)(128)(4,1)S(1)} %get-tuple-element.269) | copy-start | bytes 100
  13.3 89.3 %copy-start.4 = (bf16[512,512]{0,1:T(8,128)(2,1)}, bf16[512,512]{0,1:T(8,128)(2,1)S(1)}, u32[]{:S(2)}) copy-start(bf16[512,512]{0,1:T(8,128)(2,1)S(1)} %copy.122) | copy-start | bytes 1572868
  59.1 0.6 copy-start.5
  63.4 8.2 copy-start.15
  70.3 0.6 copy-start.8
  73.2 37.8 %copy-start.7 = (bf16[32,2,32]{2,1,0:T(2,128)(2,1)S(1)}, bf16[32,2,32]{2,1,0:T(2,128)(2,1)}, u32[]{:S(2)}) copy-start(bf16[32,2,32]{2,1,0:T(2,128)(2,1)} %copy-done.6) | copy-start | bytes 12292
  73.2 37.8 %copy-start.9 = (bf16[32,2,32]{2,1,0:T(2,128)(2,1)S(1)}, bf16[32,2,32]{2,1,0:T(2,128)(2,1)}, u32[]{:S(2)}) copy-start(bf16[32,2,32]{2,1,0:T(2,128)(2,1)} %copy-done.8) | copy-start | bytes 12292
  83.5 82.1 %copy-start.10 = (bf16[1,2048]{1,0:T(2,128)(2,1)S(1)}, bf16[1,2048]{1,0:T(2,128)(2,1)}, u32[]{:S(2)}) copy-start(bf16[1,2048]{1,0:T(2,128)(2,1)} %param.20) | copy-start | bytes 12292
  85.1 26.3 %copy-start.12 = (bf16[8,2,512]{2,0,1:T(8,128)(2,1)S(1)}, bf16[8,2,512]{2,0,1:T(8,128)(2,1)}, u32[]{:S(2)}) copy-start(bf16[8,2,512]{2,0,1:T(8,128)(2,1)} %dynamic-slice_bitcast_fusion) | copy-start | bytes 49156
  85.1 50.2 %copy-start.17 = (f32[32,6]{0,1:T(8,128)S(1)}, f32[32,6]{0,1:T(8,128)}, u32[]{:S(2)}) copy-start(f32[32,6]{0,1:T(8,128)} %param.31) | copy-start | bytes 2308
  85.1 50.5 %copy-start.18 = (u32[32]{0:T(128)S(1)}, u32[32]{0:T(128)}, u32[]{:S(2)}) copy-start(u32[32]{0:T(128)} %constant.215) | copy-start | bytes 388
  85.1 83.3 %copy-start.13 = (f32[2048]{0:T(1024)S(1)}, f32[2048]{0:T(1024)}, u32[]{:S(2)}) copy-start(f32[2048]{0:T(1024)} %param.29) | copy-start | bytes 24580
  102.6 0.8 copy-start.3
  114.4 152.3 %all-reduce.12.cloned.1.call-start = ((), (), s32[]{:S(2)}) async-start(), calls=%async_computation.6 | async-start | bytes 1622016 | tf_op jit(solution)/shard_map/psum | solution.py:247
  220.9 104.4 %all-reduce.10.cloned.1.call-start = ((), (), s32[]{:S(2)}) async-start(), calls=%async_computation.5 | async-start | bytes 131072
  266.8 58.5 %copy-start.11 = (f32[2,4,2816]{2,1,0:T(4,128)S(1)}, f32[2,4,2816]{2,1,0:T(4,128)}, u32[]{:S(2)}) copy-start(f32[2,4,2816]{2,1,0:T(4,128)} %get-tuple-element.256) | copy-start | bytes 270340
  327.1 18.1 %all-to-all-start = ((f32[4,1,512]{2,1,0:T(1,128)}), f32[4,1,512]{2,1,0:T(1,128)S(1)}, u32[]{:S(2)}, u32[]{:S(2)}) async-start(f32[4,1,512]{2,1,0:T(1,128)} %copy.144), calls=%async_computation | async-start | bytes 16384 | tf_op jit(solution)/shard_map/all_to_all | solution.py:256
  345.2 356.0 %all-to-all-start.1 = ((bf16[4,2816,512]{2,0,1:T(4,128)(2,1)}), bf16[4,2816,512]{2,0,1:T(4,128)(2,1)}, u32[]{:S(2)}, u32[]{:S(2)}) async-start(bf16[4,2816,512]{2,0,1:T(4,128)(2,1)} %bitcast.213), calls=%async_computation.1 | async-start | bytes 23068672 | tf_op jit(solution)/shard_map/all_to_all | solution.py:264
  353.8 9.9 %copy-start.2 = (s32[8,4]{0,1:T(4,128)S(1)}, s32[8,4]{0,1:T(4,128)}, u32[]{:S(2)}) copy-start(s32[8,4]{0,1:T(4,128)} %param.33) | copy-start | bytes 388
  353.8 9.9 %copy-start.14 = (s32[8,4]{0,1:T(4,128)S(1)}, s32[8,4]{0,1:T(4,128)}, u32[]{:S(2)}) copy-start(s32[8,4]{0,1:T(4,128)} %param.32) | copy-start | bytes 388
  359.0 6.7 collective-permute-start
  359.4 193.5 %collective-permute-start.1 = (bf16[4,176,512]{2,1,0:T(8,128)(2,1)}, bf16[4,176,512]{2,1,0:T(8,128)(2,1)}, u32[]{:S(2)}, u32[]{:S(2)}) collective-permute-start(bf16[4,176,512]{2,1,0:T(8,128)(2,1)} %get-tuple-element.276), channel_id=1, source_target_pairs={{0,2},{1,3},{2,0},{3,1},{4,6},{5,7},{6,4},{7,5},{8,10},{9,11},{10,... | collective-permute-start | bytes 2162696 | tf_op jit(solution)/shard_map/ppermute | solution.py:100
  361.1 207.2 %collective-permute-start.2 = (bf16[4,176,512]{2,1,0:T(8,128)(2,1)}, bf16[4,176,512]{2,1,0:T(8,128)(2,1)S(1)}, u32[]{:S(2)}, u32[]{:S(2)}) collective-permute-start(bf16[4,176,512]{2,1,0:T(8,128)(2,1)} %get-tuple-element.275), channel_id=1, source_target_pairs={{0,3},{1,2},{2,1},{3,0},{4,7},{5,6},{6,5},{7,4},{8,11},{9,10},{10,... | collective-permute-start | bytes 2162696 | tf_op jit(solution)/shard_map/ppermute | solution.py:100
  361.1 318.4 %collective-permute-start.3 = (bf16[4,176,512]{2,1,0:T(8,128)(2,1)}, bf16[4,176,512]{2,1,0:T(8,128)(2,1)S(1)}, u32[]{:S(2)}, u32[]{:S(2)}) collective-permute-start(bf16[4,176,512]{2,1,0:T(8,128)(2,1)} %get-tuple-element.274), channel_id=1, source_target_pairs={{0,4},{1,5},{2,6},{3,7},{4,0},{5,1},{6,2},{7,3},{8,12},{9,13},{10,... | collective-permute-start | bytes 2162696 | tf_op jit(solution)/shard_map/ppermute | solution.py:100
  363.7 330.3 %collective-permute-start.4 = (bf16[4,176,512]{2,1,0:T(8,128)(2,1)}, bf16[4,176,512]{2,1,0:T(8,128)(2,1)S(1)}, u32[]{:S(2)}, u32[]{:S(2)}) collective-permute-start(bf16[4,176,512]{2,1,0:T(8,128)(2,1)} %get-tuple-element.273), channel_id=1, source_target_pairs={{0,5},{1,4},{2,7},{3,6},{4,1},{5,0},{6,3},{7,2},{8,13},{9,12},{10,... | collective-permute-start | bytes 2162696 | tf_op jit(solution)/shard_map/ppermute | solution.py:100
  365.7 329.2 %collective-permute-start.5 = (bf16[4,176,512]{2,1,0:T(8,128)(2,1)}, bf16[4,176,512]{2,1,0:T(8,128)(2,1)S(1)}, u32[]{:S(2)}, u32[]{:S(2)}) collective-permute-start(bf16[4,176,512]{2,1,0:T(8,128)(2,1)} %get-tuple-element.272), channel_id=1, source_target_pairs={{0,6},{1,7},{2,4},{3,5},{4,2},{5,3},{6,0},{7,1},{8,14},{9,15},{10,... | collective-permute-start | bytes 2162696 | tf_op jit(solution)/shard_map/ppermute | solution.py:100
  552.9 143.0 %collective-permute-start.6 = (bf16[4,176,512]{2,1,0:T(8,128)(2,1)}, bf16[4,176,512]{2,1,0:T(8,128)(2,1)S(1)}, u32[]{:S(2)}, u32[]{:S(2)}) collective-permute-start(bf16[4,176,512]{2,1,0:T(8,128)(2,1)} %get-tuple-element.271), channel_id=1, source_target_pairs={{0,7},{1,6},{2,5},{3,4},{4,3},{5,2},{6,1},{7,0},{8,15},{9,14},{10,... | collective-permute-start | bytes 2162696 | tf_op jit(solution)/shard_map/ppermute | solution.py:100
  701.1 66.1 %all-to-all-start.3 = ((bf16[8,176,512]{2,1,0:T(8,128)(2,1)}), bf16[8,176,512]{2,1,0:T(8,128)(2,1)S(1)}, u32[]{:S(2)}, u32[]{:S(2)}) async-start(bf16[8,176,512]{2,1,0:T(8,128)(2,1)} %gather_fusion.5), calls=%async_computation.3 | async-start | bytes 2883584 | tf_op jit(solution)/shard_map/all_to_all | solution.py:270
  767.3 70.4 %all-to-all-start.2 = ((bf16[8,352,512]{2,1,0:T(8,128)(2,1)}), bf16[8,352,512]{2,1,0:T(8,128)(2,1)}, u32[]{:S(2)}, u32[]{:S(2)}) async-start(bf16[8,352,512]{2,1,0:T(8,128)(2,1)} %gather_fusion.4), calls=%async_computation.2 | async-start | bytes 5767168 | tf_op jit(solution)/shard_map/all_to_all | solution.py:269
  837.7 10.8 %copy-start.1 = (bf16[2816,512]{1,0:T(8,128)(2,1)S(1)}, bf16[2816,512]{1,0:T(8,128)(2,1)}, u32[]{:S(2)}) copy-start(bf16[2816,512]{1,0:T(8,128)(2,1)} %param.37) | copy-start | bytes 8650756
  (1 other events, 0.6 us)
Sparse Core Ops, SparseCore 0:
  114.6 51.0 all-reduce.7
  221.0 45.6 all-reduce.11
  271.6 53.6 all-reduce.9
